TPU v7x, 32 devices: a whole 2x2x4 slice. The times are simulated.
32 devices in a mesh: ang: 8 (over z, core), row: 4 (over y, x).
Axes of the slice: x: 2, y: 2, z: 4, core: 2. Of those that a mesh axis runs over, the one named last changes fastest.
Arguments:
- panels: bfloat16 [4, 32, 64, 2, 128], P('row', None, 'ang'), may hold values from -6 to 6
- panel_slot: int32 [4, 32], P('row'), may hold values from 0 to 15
- panel_cell: int32 [4, 32, 2], P('row'), may hold values from 0 to 15
- bloch_k: float32 [8, 2], replicated, may hold values from -3.140625 to 3.140625
- leaf_inverse: bfloat16 [8, 2, 8192, 256], P('ang', None, 'row'), may hold values from -0.25 to 0.25
- level_left: bfloat16 [8, 3, 2, 32, 8192], P('ang', None, None, None, 'row'), may hold values from -0.75 to 0.75
- level_right: bfloat16 [8, 3, 2, 32, 8192], P('ang', None, None, None, 'row'), may hold values from -0.125 to 0.125
- block_left: bfloat16 [8, 2, 32, 8192], P('ang', None, None, 'row'), may hold values from -0.75 to 0.75
- block_right: bfloat16 [8, 2, 32, 8192], P('ang', None, None, 'row'), may hold values from -0.09375 to 0.09375
- block_coupling: bfloat16 [8, 4, 2, 32, 128], P('ang', 'row'), may hold values from -0.375 to 0.375
- rank_count: int32 [8, 4], P('ang', 'row'), may hold values from 16 to 32
- quad_weight: float32 [8, 2], P('ang'), may hold values from -2 to 2
Outputs:
- response: float32 [64, 2, 8192], P('ang', None, 'row')
All inputs are finite; a program needn't handle non-finite values.
Results may differ from a plain program's by a relative error of at most 0.0045.
Values may be sent and summed in bfloat16 or wider, within the bound.
No kernel may reach another device: no remote copies, remote signals or barrier semaphores. Data moves between devices by JAX's collectives and lax.ppermute only.
A program may use at most 64 MiB of HBM per device.

v0:
```python
import jax
import jax.numpy as jnp
from jax import lax
from jax.sharding import PartitionSpec as P


def complex_product(form, left_real, left_imag, right_real, right_imag):

    def single(first, second):
        return jnp.einsum(form, first, second, preferred_element_type=jnp.float32)

    return (
        single(left_real, right_real) - single(left_imag, right_imag),
        single(left_real, right_imag) + single(left_imag, right_real),
    )


def assemble(phase_cosine, phase_sin, onehot, panel_group):
    coef_cos = phase_cosine[:, :, None] * onehot[None]
    coef_sin = phase_sin[:, :, None] * onehot[None]
    panel_real = panel_group[:, :, 0]
    panel_imag = panel_group[:, :, 1]

    def single(coefficient, entry_values):
        return jnp.einsum(
            "aqk,qsw->askw", coefficient, entry_values, preferred_element_type=jnp.float32
        )

    real_part = single(coef_cos, panel_real) + single(coef_sin, panel_imag)
    imag_part = single(coef_cos, panel_imag) - single(coef_sin, panel_real)
    stacked = jnp.stack([real_part, imag_part], 2)
    dims = stacked.shape
    return stacked.reshape(dims[0], dims[1], 2, dims[3] * dims[4]).astype(jnp.bfloat16)


def near_field(excite, leaf_block, right_factors, left_factors):
    source_count = excite.shape[0]
    row_count = excite.shape[2]
    leaf_width = leaf_block.shape[2]
    leaf_count = row_count // leaf_width
    rank_width = right_factors.shape[2]
    gathered_groups = excite.reshape(source_count, 2, leaf_count, leaf_width)
    real_part, imag_part = complex_product(
        "lwv,slv->slw",
        leaf_block[0].reshape(leaf_count, leaf_width, leaf_width),
        leaf_block[1].reshape(leaf_count, leaf_width, leaf_width),
        gathered_groups[:, 0],
        gathered_groups[:, 1],
    )
    real_part = real_part.reshape(source_count, row_count)
    imag_part = imag_part.reshape(source_count, row_count)
    for tree_level_index in range(right_factors.shape[0]):
        node_size = row_count // 2 ** (tree_level_index + 1)
        groups = row_count // node_size
        node_view = excite.reshape(source_count, 2, groups, node_size)
        right_real = right_factors[tree_level_index, 0].reshape(rank_width, groups, node_size)
        right_imag = right_factors[tree_level_index, 1].reshape(rank_width, groups, node_size)
        proj_real, proj_imag = complex_product(
            "rgm,sgm->sgr", right_real, right_imag, node_view[:, 0], node_view[:, 1]
        )
        projected = jnp.stack([proj_real, proj_imag], 1).astype(jnp.bfloat16)
        swapped = projected.reshape(source_count, 2, groups // 2, 2, rank_width)[
            :, :, :, ::-1
        ].reshape(source_count, 2, groups, rank_width)
        left_real = left_factors[tree_level_index, 0].reshape(rank_width, groups, node_size)
        left_imag = left_factors[tree_level_index, 1].reshape(rank_width, groups, node_size)
        add_real, add_imag = complex_product(
            "rgm,sgr->sgm", left_real, left_imag, swapped[:, 0], swapped[:, 1]
        )
        real_part = real_part + add_real.reshape(source_count, row_count)
        imag_part = imag_part + add_imag.reshape(source_count, row_count)
    return (real_part, imag_part)


def shards(
    panels,
    panel_slot,
    panel_cell,
    bloch_k,
    leaf_inverse,
    level_left,
    level_right,
    block_left,
    block_right,
    block_coupling,
    rank_count,
    quad_weight,
):
    local_angles = leaf_inverse.shape[0]
    row_count = leaf_inverse.shape[2]
    panel_width = panels.shape[4]
    slot_count = row_count // panel_width
    onehot = (panel_slot[0][:, None] == jnp.arange(slot_count, dtype=jnp.int32)[None, :]).astype(
        jnp.bfloat16
    )
    cell_float = panel_cell[0].astype(jnp.float32)
    own_wave = lax.dynamic_slice_in_dim(
        bloch_k, lax.axis_index("ang") * local_angles, local_angles, 0
    )
    theta = own_wave[:, 0:1] * cell_float[None, :, 0] + own_wave[:, 1:2] * cell_float[None, :, 1]
    own_cos = jnp.cos(theta).astype(jnp.bfloat16)
    own_sin = jnp.sin(theta).astype(jnp.bfloat16)
    excitation = assemble(
        own_cos, own_sin, onehot, lax.all_gather(panels, "ang", axis=2, tiled=True)[0]
    )
    rank_width = block_right.shape[2]
    rank_iota = jnp.arange(rank_width, dtype=jnp.int32)
    rank_masks = (rank_iota[None, :] < rank_count).astype(jnp.bfloat16)
    right_masked = block_right * rank_masks[:, None, :, None]
    left_masked = block_left * rank_masks[:, None, :, None]
    proj_real, proj_imag = complex_product(
        "arm,asm->asr",
        right_masked[:, 0],
        right_masked[:, 1],
        excitation[:, :, 0],
        excitation[:, :, 1],
    )
    projected = jnp.stack([proj_real, proj_imag], 2).astype(jnp.bfloat16)
    gathered = lax.all_gather(projected[:, None], "row", axis=1, tiled=True)
    number_of_blocks = gathered.shape[1]
    keep_other = (jnp.arange(number_of_blocks, dtype=jnp.int32) != lax.axis_index("row")).astype(
        jnp.bfloat16
    )
    gathered = gathered * keep_other[None, :, None, None, None]
    coupling = block_coupling[:, 0].reshape(
        local_angles, 2, rank_width, number_of_blocks, rank_width
    )
    coup_real, coup_imag = complex_product(
        "arjq,ajsq->asr", coupling[:, 0], coupling[:, 1], gathered[:, :, :, 0], gathered[:, :, :, 1]
    )
    coupled = jnp.stack([coup_real, coup_imag], 2).astype(jnp.bfloat16)
    excite_part = excitation[0]
    coupled_part = coupled[0]
    near_real, near_imag = near_field(excite_part, leaf_inverse[0], level_right[0], level_left[0])
    far_real, far_imag = complex_product(
        "rm,sr->sm", left_masked[0, 0], left_masked[0, 1], coupled_part[:, 0], coupled_part[:, 1]
    )
    field_real = near_real + far_real
    field_imag = near_imag + far_imag
    weight_real = quad_weight[0, 0]
    weight_imag = quad_weight[0, 1]
    summed = jnp.stack(
        [
            weight_real * field_real - weight_imag * field_imag,
            weight_real * field_imag + weight_imag * field_real,
        ],
        1,
    )
    return lax.psum_scatter(summed, "ang", scatter_dimension=0, tiled=True)


def solution(mesh):
    placed = (
        P("row", None, "ang", None, None),
        P("row", None),
        P("row", None, None),
        P(),
        P("ang", None, "row", None),
        P("ang", None, None, None, "row"),
        P("ang", None, None, None, "row"),
        P("ang", None, None, "row"),
        P("ang", None, None, "row"),
        P("ang", "row", None, None, None),
        P("ang", "row"),
        P("ang", None),
    )
    return jax.shard_map(
        shards, mesh=mesh, in_specs=placed, out_specs=P("ang", None, "row"), check_vma=False
    )
```

profile of v0, /device:TPU:0, one launch (start us, length us, event | category | flops | bytes accessed | tf_op | source)
XLA Modules:
  0.0 121.3 jit_solution(7901270127954322322)
XLA Ops:
  6.5 1.7 %copy.87 = bf16[1,32,8,2,128]{4,1,2,3,0:T(8,128)(2,1)} copy(bf16[1,32,8,2,128]{4,3,2,1,0:T(2,128)(2,1)} %param.12) | data formatting | bytes 262144 | tf_op args[0]
  9.0 1.3 %fusion.122 = (bf16[1,1,32,2048]{3,2,1,0:T(8,128)(2,1)S(1)}, bf16[1,1,32,2048]{3,2,1,0:T(8,128)(2,1)S(1)}, bf16[1,1,32,2048]{3,2,1,0:T(8,128)(2,1)S(1)}, bf16[1,...) fusion(bf16[3,2,32,2048]{3,2,1,0:T(8,128)(2,1)} %bitcast.282), kind=kLoop, calls=%fused_computation.173 | loop fusion | bytes 1572864 | tf_op jit(solution)/shard_map/slice | solution.py:57
  20.3 1.3 %convert_bitcast_fusion.1 = (bf16[32]{0:T(256)(128)(2,1)S(1)}, f32[32,1]{0,1:T(1,128)S(1)}) fusion(f32[32,2]{0,1:T(2,128)S(1)} %convert_bitcast_fusion, f32[]{:T(128)} %bitcast.4, f32[]{:T(128)} %bitcast.2), kind=kLoop, calls=%fused_computation.163 | loop fusion | flops 128 | bytes 456 | tf_op jit(solution)/shard_map/convert_element_type | solution.py:102
  22.3 0.9 broadcast_multiply_fusion
  23.2 1.7 %fusion.120 = (bf16[1,1,2048,256]{3,2,1,0:T(8,128)(2,1)S(1)}, bf16[1,1,2048,256]{3,2,1,0:T(8,128)(2,1)S(1)}) fusion(bf16[1,2,2048,256]{3,2,1,0:T(8,128)(2,1)} %param.16), kind=kLoop, calls=%fused_computation.171 | loop fusion | bytes 4194304 | tf_op jit(solution)/shard_map/slice | solution.py:46
  24.9 8.9 %all-gather.2.cloned.1.call-done = bf16[1,32,64,2,128]{4,1,2,3,0:T(8,128)(2,1)} async-done(((bf16[1,32,8,2,128]{4,1,2,3,0:T(8,128)(2,1)}), bf16[1,32,64,2,128]{4,1,2,3,0:T(8,128)(2,1)}) %all-gather.2.cloned.1.call-update) | async-done | bytes 1048592 | tf_op jit(solution)/shard_map/all_gather | solution.py:104
  33.9 1.3 %fusion.28 = f32[16,64,128]{2,0,1:T(8,128)S(1)} fusion(bf16[32,64,2,128]{3,0,1,2:T(8,128)(2,1)} %bitcast.250, s32[32]{0:T(128)S(1)} %bitcast.298, bf16[32]{0:T(256)(128)(2,1)S(1)} %convert_bitcast_fusion.2), kind=kOutput, calls=%fused_computation.57 | convolution fusion | flops 8389632 | bytes 1048768 | tf_op jit(solution)/shard_map/aqk,qsw->askw/dot_general | solution.py:25
  35.2 2.1 %fusion.29 = f32[16,64,128]{2,0,1:T(8,128)} fusion(bf16[32,64,2,128]{3,0,1,2:T(8,128)(2,1)} %bitcast.251, s32[32]{0:T(128)S(1)} %bitcast.299, bf16[32]{0:T(256)(128)(2,1)S(1)} %convert_bitcast_fusion.2), kind=kOutput, calls=%fused_computation.58 | convolution fusion | flops 8389632 | bytes 1048768 | tf_op jit(solution)/shard_map/aqk,qsw->askw/dot_general | solution.py:25
  39.0 2.0 %fusion.11 = bf16[16,64,128]{2,0,1:T(8,128)(2,1)} fusion(f32[16,64,128]{2,0,1:T(8,128)} %fusion.29, bf16[32,64,2,128]{3,0,1,2:T(8,128)(2,1)S(1)} %bitcast.253, s32[32]{0:T(128)S(1)} %bitcast.301, bf16[32]{0:T(256)(128)(2,1)S(1)} %get-tuple-element.5), kind=kOutput, calls=%fused_computation.23 | convolution fusion | flops 8651776 | bytes 1311744 | tf_op jit(solution)/shard_map/aqk,qsw->askw/dot_general | solution.py:25
  41.0 1.1 squeeze.95
  42.1 1.7 %squeeze.90 = bf16[64,2,1024]{2,1,0:T(2,128)(2,1)} reshape(bf16[1,64,16,128]{3,2,1,0:T(8,128)(2,1)} %bitcast.260) | data formatting | bytes 524288 | tf_op jit(solution)/shard_map/squeeze | solution.py:59
  43.9 1.2 fusion.44
  45.1 1.1 fusion.40
  46.7 1.1 fusion.78
  47.8 1.1 fusion.80
  49.1 1.1 fusion.34
  50.2 1.1 fusion.30
  51.3 1.1 fusion.27
  52.4 1.1 fusion.26
  53.6 8.2 %all_gather.7 = bf16[1,4,64,2,32]{2,4,3,0,1:T(8,128)(2,1)S(1)} all-gather(bf16[1,1,64,2,32]{2,4,3,0,1:T(8,128)(2,1)S(1)} %maximum_bitcast_fusion), channel_id=1, replica_groups=mesh['ang'=8,'row'=4] {'row'}, dimensions={1}, use_global_device_ids=true | all-gather | bytes 40960 | tf_op jit(solution)/shard_map/all_gather | solution.py:119
  61.8 1.5 %convolution_bitcast_fusion = f32[64,32]{0,1:T(8,128)} fusion(bf16[1,1,32,4,32]{4,3,2,1,0:T(4,128)(2,1)} %get-tuple-element.24, bf16[1,4,64,2,32]{2,4,1,3,0:T(8,128)(2,1)S(1)} %copy_multiply_fusion), kind=kOutput, calls=%fused_computation.36 | convolution fusion | flops 524288 | bytes 49152 | tf_op jit(solution)/shard_map/arjq,ajsq->asr/dot_general | solution.py:10
  63.3 1.5 %convolution_bitcast_fusion.2 = f32[64,32]{0,1:T(8,128)} fusion(bf16[1,1,32,4,32]{4,3,2,1,0:T(4,128)(2,1)} %get-tuple-element.24, bf16[1,4,64,2,32]{2,4,1,3,0:T(8,128)(2,1)S(1)} %copy_multiply_fusion), kind=kOutput, calls=%fused_computation.38 | convolution fusion | flops 524288 | bytes 49152 | tf_op jit(solution)/shard_map/arjq,ajsq->asr/dot_general | solution.py:10
  64.9 1.1 fusion.60
  66.0 1.1 fusion.54
  67.6 1.1 fusion.70
  68.7 1.1 fusion.68
  69.8 1.2 %fusion.62 = f32[8,64,256]{2,1,0:T(8,128)} fusion(bf16[8,256,256]{2,1,0:T(8,128)(2,1)S(1)} %bitcast.246, bf16[64,8,256]{2,1,0:T(8,128)(2,1)S(1)} %squeeze.86), kind=kOutput, calls=%fused_computation.91 | convolution fusion | flops 67108864 | bytes 1835008 | tf_op jit(solution)/shard_map/lwv,slv->slw/dot_general | solution.py:10
  71.0 1.2 %fusion.52 = f32[8,64,256]{2,1,0:T(8,128)} fusion(bf16[8,256,256]{2,1,0:T(8,128)(2,1)S(1)} %bitcast.247, bf16[64,8,256]{2,1,0:T(8,128)(2,1)S(1)} %squeeze.87), kind=kOutput, calls=%fused_computation.81 | convolution fusion | flops 67108864 | bytes 1835008 | tf_op jit(solution)/shard_map/lwv,slv->slw/dot_general | solution.py:10
  78.9 1.7 %subtract_bitcast_fusion = (f32[64,1,2048]{2,0,1:T(8,128)S(1)}, f32[64,1,2048]{2,0,1:T(8,128)S(1)}) fusion(f32[64,2048]{1,0:T(8,128)S(1)} %fusion, f32[]{:T(128)} %bitcast.66, f32[]{:T(128)} %bitcast, f32[64,2048]{1,0:T(8,128)S(1)} %fusion.64, bf16[64,32]{0,1:T(8,128)(2,1)S(1)} %fusion.23, bf16[1,2,32,2048]{3,2,1,0:T(8,128)(2,1)S(1)} %copy-done.3, ...), kind=kOutput, calls=%fused_computation.56 | convolution fusion | flops 9830400 | bytes 4333576 | tf_op jit(solution)/shard_map/rm,sr->sm/dot_general | solution.py:10
  80.6 1.1 pad_maximum_fusion
  81.7 31.1 %reduce-scatter.2.cloned.1.call-done = f32[8,2,2048]{2,0,1:T(8,128)} async-done(((f32[64,2,2048]{2,0,1:T(8,128)}), f32[8,2,2048]{2,0,1:T(8,128)}) %reduce-scatter.2.cloned.1.call-update) | async-done | bytes 131088 | tf_op jit(solution)/shard_map/reduce_scatter | solution.py:149
  112.8 1.7 %copy.140 = f32[8,2,2048]{2,1,0:T(2,128)} copy(f32[8,2,2048]{2,0,1:T(8,128)} %reduce-scatter.2.cloned.1.call-done) | data formatting | bytes 262144 | tf_op jit(solution)/shard_map/reduce_scatter | solution.py:149
  (152 shorter events, 20.1 us)
Async XLA Ops:
  6.5 5.2 %copy-start = (f32[8,2]{0,1:T(2,128)S(1)}, f32[8,2]{0,1:T(2,128)}, u32[]{:S(2)}) copy-start(f32[8,2]{0,1:T(2,128)} %param.15) | copy-start | bytes 196
  6.5 3.7 %copy-start.18 = (bf16[1,3,2,32,2048]{4,3,2,1,0:T(8,128)(2,1)S(1)}, bf16[1,3,2,32,2048]{4,3,2,1,0:T(8,128)(2,1)}, u32[]{:S(2)}) copy-start(bf16[1,3,2,32,2048]{4,3,2,1,0:T(8,128)(2,1)} %param.17) | copy-start | bytes 2359300
  6.5 4.5 %copy-start.40 = (f32[1,2]{1,0:T(1,128)S(1)}, f32[1,2]{1,0:T(1,128)}, u32[]{:S(2)}) copy-start(f32[1,2]{1,0:T(1,128)} %param.23) | copy-start | bytes 28
  6.5 27.3 %all-gather.2.cloned.1.call-start = ((), (), s32[]{:S(2)}) async-start(), calls=%async_computation.1 | async-start | bytes 1179648 | tf_op jit(solution)/shard_map/all_gather | solution.py:104
  8.2 104.6 %reduce-scatter.2.cloned.1.call-start = ((), (), s32[]{:S(2)}) async-start(), calls=%async_computation.2 | async-start | bytes 1179648 | tf_op jit(solution)/shard_map/reduce_scatter | solution.py:149
  10.2 9.4 %copy-start.38 = (bf16[1,1,2,32,128]{4,3,2,1,0:T(8,128)(2,1)S(1)}, bf16[1,1,2,32,128]{4,3,2,1,0:T(8,128)(2,1)}, u32[]{:S(2)}) copy-start(bf16[1,1,2,32,128]{4,3,2,1,0:T(8,128)(2,1)} %param.21) | copy-start | bytes 49156
  10.3 12.0 %copy-start.29 = (bf16[1,2,32,2048]{3,2,1,0:T(8,128)(2,1)S(1)}, bf16[1,2,32,2048]{3,2,1,0:T(8,128)(2,1)}, u32[]{:S(2)}) copy-start(bf16[1,2,32,2048]{3,2,1,0:T(8,128)(2,1)} %param.19) | copy-start | bytes 786436
  10.3 12.0 %copy-start.30 = (bf16[1,2,32,2048]{3,2,1,0:T(8,128)(2,1)S(1)}, bf16[1,2,32,2048]{3,2,1,0:T(8,128)(2,1)}, u32[]{:S(2)}) copy-start(bf16[1,2,32,2048]{3,2,1,0:T(8,128)(2,1)} %param.20) | copy-start | bytes 786436
  23.2 10.6 %copy-start.39 = (s32[1,32]{1,0:T(1,128)S(1)}, s32[1,32]{1,0:T(1,128)}, u32[]{:S(2)}) copy-start(s32[1,32]{1,0:T(1,128)} %param.13) | copy-start | bytes 388
  33.8 3.4 %copy-start.1 = (bf16[1,32,64,2,128]{4,1,2,3,0:T(8,128)(2,1)S(1)}, bf16[1,32,64,2,128]{4,1,2,3,0:T(8,128)(2,1)}, u32[]{:S(2)}) copy-start(bf16[1,32,64,2,128]{4,1,2,3,0:T(8,128)(2,1)} %all-gather.2.cloned.1.call-done) | copy-start | bytes 3145732
  41.0 5.2 %copy-start.35 = (bf16[32,4,512]{2,1,0:T(4,128)(2,1)S(1)}, bf16[32,4,512]{2,1,0:T(4,128)(2,1)}, u32[]{:S(2)}) copy-start(bf16[32,4,512]{2,1,0:T(4,128)(2,1)} %reshape_squeeze.56) | copy-start | bytes 393220
  41.0 5.4 %copy-start.28 = (bf16[64,4,512]{2,1,0:T(4,128)(2,1)S(1)}, bf16[64,4,512]{2,1,0:T(4,128)(2,1)}, u32[]{:S(2)}) copy-start(bf16[64,4,512]{2,1,0:T(4,128)(2,1)} %squeeze.94) | copy-start | bytes 786436
  41.0 5.7 %copy-start.15 = (bf16[32,4,512]{2,1,0:T(4,128)(2,1)S(1)}, bf16[32,4,512]{2,1,0:T(4,128)(2,1)}, u32[]{:S(2)}) copy-start(bf16[32,4,512]{2,1,0:T(4,128)(2,1)} %reshape_squeeze.57) | copy-start | bytes 393220
  43.9 5.1 %copy-start.2 = (bf16[16,64,128]{2,0,1:T(8,128)(2,1)S(1)}, bf16[16,64,128]{2,0,1:T(8,128)(2,1)}, u32[]{:S(2)}) copy-start(bf16[16,64,128]{2,0,1:T(8,128)(2,1)} %fusion.11) | copy-start | bytes 786436
  46.7 2.2 %copy-start.21 = (bf16[64,2,2,2,32]{0,4,3,2,1:T(8,128)(2,1)}, bf16[64,2,2,2,32]{0,4,3,2,1:T(8,128)(2,1)S(1)}, u32[]{:S(2)}) copy-start(bf16[64,2,2,2,32]{0,4,3,2,1:T(8,128)(2,1)S(1)} %rev.7) | copy-start | bytes 98308
  48.9 18.2 %copy-start.14 = (bf16[4,8,8,256]{3,2,1,0:T(8,128)(2,1)S(1)}, bf16[4,8,8,256]{3,2,1,0:T(8,128)(2,1)}, u32[]{:S(2)}) copy-start(bf16[4,8,8,256]{3,2,1,0:T(8,128)(2,1)} %copy.152) | copy-start | bytes 393220
  51.3 16.4 %copy-start.13 = (bf16[4,8,8,256]{3,2,1,0:T(8,128)(2,1)S(1)}, bf16[4,8,8,256]{3,2,1,0:T(8,128)(2,1)}, u32[]{:S(2)}) copy-start(bf16[4,8,8,256]{3,2,1,0:T(8,128)(2,1)} %copy.153) | copy-start | bytes 393220
  61.8 8.0 %copy-start.19 = (bf16[1,4,64,2,32]{2,4,1,3,0:T(8,128)(2,1)}, bf16[1,4,64,2,32]{2,4,1,3,0:T(8,128)(2,1)S(1)}, u32[]{:S(2)}) copy-start(bf16[1,4,64,2,32]{2,4,1,3,0:T(8,128)(2,1)S(1)} %copy_multiply_fusion) | copy-start | bytes 98308
  67.6 4.7 %copy-start.16 = (bf16[64,2,4,2,32]{0,4,3,2,1:T(8,128)(2,1)}, bf16[64,2,4,2,32]{0,4,3,2,1:T(8,128)(2,1)S(1)}, u32[]{:S(2)}) copy-start(bf16[64,2,4,2,32]{0,4,3,2,1:T(8,128)(2,1)S(1)} %rev.8) | copy-start | bytes 196612
  68.7 3.6 %copy-start.5 = (f32[4,64,512]{2,1,0:T(8,128)S(1)}, f32[4,64,512]{2,1,0:T(8,128)}, u32[]{:S(2)}) copy-start(f32[4,64,512]{2,1,0:T(8,128)} %fusion.78) | copy-start | bytes 1572868
  68.7 3.6 %copy-start.11 = (bf16[32,4,512]{2,1,0:T(4,128)(2,1)S(1)}, bf16[32,4,512]{2,1,0:T(4,128)(2,1)}, u32[]{:S(2)}) copy-start(bf16[32,4,512]{2,1,0:T(4,128)(2,1)} %reshape_squeeze.58) | copy-start | bytes 393220
  68.7 3.6 %copy-start.22 = (bf16[64,2,2,2,32]{0,4,3,2,1:T(8,128)(2,1)S(1)}, bf16[64,2,2,2,32]{0,4,3,2,1:T(8,128)(2,1)}, u32[]{:S(2)}) copy-start(bf16[64,2,2,2,32]{0,4,3,2,1:T(8,128)(2,1)} %copy-done.21) | copy-start | bytes 98308
  71.0 1.6 %copy-start.25 = (bf16[64,2,1024]{2,1,0:T(2,128)(2,1)S(1)}, bf16[64,2,1024]{2,1,0:T(2,128)(2,1)}, u32[]{:S(2)}) copy-start(bf16[64,2,1024]{2,1,0:T(2,128)(2,1)} %squeeze.88) | copy-start | bytes 786436
  71.0 1.6 %copy-start.34 = (bf16[32,2,1024]{2,1,0:T(2,128)(2,1)S(1)}, bf16[32,2,1024]{2,1,0:T(2,128)(2,1)}, u32[]{:S(2)}) copy-start(bf16[32,2,1024]{2,1,0:T(2,128)(2,1)} %reshape_squeeze.51) | copy-start | bytes 393220
  71.0 1.8 %copy-start.27 = (bf16[64,2,1024]{2,1,0:T(2,128)(2,1)S(1)}, bf16[64,2,1024]{2,1,0:T(2,128)(2,1)}, u32[]{:S(2)}) copy-start(bf16[64,2,1024]{2,1,0:T(2,128)(2,1)} %squeeze.90) | copy-start | bytes 786436
  72.3 1.4 %copy-start.12 = (bf16[32,2,1024]{2,1,0:T(2,128)(2,1)S(1)}, bf16[32,2,1024]{2,1,0:T(2,128)(2,1)}, u32[]{:S(2)}) copy-start(bf16[32,2,1024]{2,1,0:T(2,128)(2,1)} %reshape_squeeze.53) | copy-start | bytes 393220
  73.4 1.2 copy-start.4
  73.4 1.2 copy-start.23
  73.4 1.5 %copy-start.31 = (bf16[64,2,32]{0,2,1:T(8,128)(2,1)}, bf16[64,2,32]{0,2,1:T(8,128)(2,1)S(1)}, u32[]{:S(2)}) copy-start(bf16[64,2,32]{0,2,1:T(8,128)(2,1)S(1)} %squeeze.91) | copy-start | bytes 24580
  74.6 1.3 %copy-start.36 = (f32[64,32]{0,1:T(8,128)S(1)}, f32[64,32]{0,1:T(8,128)}, u32[]{:S(2)}) copy-start(f32[64,32]{0,1:T(8,128)} %convolution_bitcast_fusion.2) | copy-start | bytes 24580
  74.6 1.5 %copy-start.8 = (f32[8,64,256]{2,1,0:T(8,128)S(1)}, f32[8,64,256]{2,1,0:T(8,128)}, u32[]{:S(2)}) copy-start(f32[8,64,256]{2,1,0:T(8,128)} %fusion.62) | copy-start | bytes 1572868
  77.0 1.2 copy-start.6
  (11 other events, 11.4 us)
Sparse Core Ops, SparseCore 0:
  9.0 24.8 all-gather.1
  81.8 30.9 reduce-scatter.1
where the time goes:
time: 122 us; the launch traced here: 121 us
  waiting for transfers between devices  40.1 us (33%)
  matrix products  31.9 us (26%)
  local copies, waits for them, and re-layouts  22.2 us (18%)
  between operations  14.7 us (12%)
  blocking collectives  8.16 us (7%)
  other arithmetic  4.16 us (3%)
    reduce_scatter x1, waiting for transfers between devices, shards(): return lax.psum_scatter(summed, 'ang', scatter_dimension=0, tiled=True)  31.1 us
    dot_general x40, matrix products, single(): return jnp.einsum(form, first, second, preferred_element_type=jnp.float32)  26.3 us
    all_gather x1, waiting for transfers between devices, shards(): lax.all_gather(panels, 'ang', axis=2, tiled=True)[0]  8.91 us
    all_gather x1, blocking collectives, shards(): gathered = lax.all_gather(projected[:, None], 'row', axis=1, tiled=True)  8.16 us
    dot_general x4, matrix products, single(): jnp.einsum('aqk,qsw->askw', coefficient, entry_values, preferred_element_...  5.57 us
    unnamed x87, local copies, waits for them, and re-layouts  5.45 us
    squeeze x2, local copies, waits for them, and re-layouts, near_field(): node_view[:, 1]  2.85 us
  transfers between devices with their start and end apart: 2, of which 2 were waited for; matrix products, arithmetic and copies ran while one was open for 13% of the time, Pallas kernels for 0%

commit v1 on v0

--- a/solution.py
+++ b/solution.py
@@ -2,6 +2,18 @@
 import jax.numpy as jnp
 from jax import lax
 from jax.sharding import PartitionSpec as P
+
+
+def doubled_up(array, axis, dim):
+    ways, here, step = (lax.axis_size(axis), lax.axis_index(axis), array.shape[dim])
+    line, have = (array, 1)
+    while have < ways:
+        line = jnp.concatenate(
+            [line, lax.ppermute(line, axis, [(d, (d - have) % ways) for d in range(ways)])],
+            axis=dim,
+        )
+        have = 2 * have
+    return jnp.roll(line, here * step, axis=dim)
 
 
 def complex_product(form, left_real, left_imag, right_real, right_imag):
@@ -100,9 +112,7 @@
     theta = own_wave[:, 0:1] * cell_float[None, :, 0] + own_wave[:, 1:2] * cell_float[None, :, 1]
     own_cos = jnp.cos(theta).astype(jnp.bfloat16)
     own_sin = jnp.sin(theta).astype(jnp.bfloat16)
-    excitation = assemble(
-        own_cos, own_sin, onehot, lax.all_gather(panels, "ang", axis=2, tiled=True)[0]
-    )
+    excitation = assemble(own_cos, own_sin, onehot, doubled_up(panels, "ang", 2)[0])
     rank_width = block_right.shape[2]
     rank_iota = jnp.arange(rank_width, dtype=jnp.int32)
     rank_masks = (rank_iota[None, :] < rank_count).astype(jnp.bfloat16)

time: 122 us -> 162 us (1.33)
  local copies, waits for them, and re-layouts: 22.2 us -> 43.3 us
  waiting for transfers between devices: 40.1 us -> 52.9 us
  starting transfers between devices: 0.04 us -> 5.79 us
  matrix products: 31.9 us -> 29.3 us
  other arithmetic: 4.16 us -> 6.56 us
    ppermute x0 -> x3, waiting for transfers between devices: none -> 21 us  [doubled_up(): lax.ppermute(line, axis, [(d, (d - have) % ways) for d in range(ways)])]
    all_gather x1 -> x0, waiting for transfers between devices: 8.91 us -> none  [shards(): lax.all_gather(panels, 'ang', axis=2, tiled=True)[0]]
    unnamed x87 -> x93, local copies, waits for them, and re-layouts: 5.45 us -> 11.8 us
    ppermute x0 -> x3, starting transfers between devices: none -> 5.79 us  [doubled_up(): lax.ppermute(line, axis, [(d, (d - have) % ways) for d in range(ways)])]
    dynamic_slice x0 -> x2, local copies, waits for them, and re-layouts: none -> 2.76 us  [doubled_up(): return jnp.roll(line, here * step, axis=dim)]
    dot_general x4, matrix products: 5.57 us -> 3.39 us  [single(): jnp.einsum('aqk,qsw->askw', coefficient, entry_values, preferred_element_...]
    squeeze x2, local copies, waits for them, and re-layouts: 1.56 us -> 3.5 us  [near_field(): node_view[:, 0]]
    another operation x2, local copies, waits for them, and re-layouts: 0.82 us -> 2.61 us  [near_field(): left_factors[tree_level_index, 1].reshape(rank_width, groups, node_size)]
  transfers between devices with their start and end apart: 2 -> 4, of which waited for: 2 -> 2; matrix products, arithmetic and copies ran while one was open for 13% -> 14% of each run, Pallas kernels for 0% -> 0%
where the time goes in v1:
time: 162 us; the launch traced here: 161 us
  waiting for transfers between devices  52.9 us (33%)
  local copies, waits for them, and re-layouts  43.3 us (27%)
  matrix products  29.3 us (18%)
  between operations  14.7 us (9%)
  blocking collectives  8.48 us (5%)
  other arithmetic  6.56 us (4%)
  starting transfers between devices  5.79 us (4%)
    reduce_scatter x1, waiting for transfers between devices, shards(): return lax.psum_scatter(summed, 'ang', scatter_dimension=0, tiled=True)  31.9 us
    dot_general x40, matrix products, single(): return jnp.einsum(form, first, second, preferred_element_type=jnp.float32)  26 us
    ppermute x3, waiting for transfers between devices, doubled_up(): lax.ppermute(line, axis, [(d, (d - have) % ways) for d in range(ways)])  21 us
    unnamed x93, local copies, waits for them, and re-layouts  11.8 us
    all_gather x1, blocking collectives, shards(): gathered = lax.all_gather(projected[:, None], 'row', axis=1, tiled=True)  8.48 us
    ppermute x3, starting transfers between devices, doubled_up(): lax.ppermute(line, axis, [(d, (d - have) % ways) for d in range(ways)])  5.79 us
    squeeze x2, local copies, waits for them, and re-layouts, near_field(): node_view[:, 0]  3.5 us
    dot_general x4, matrix products, single(): jnp.einsum('aqk,qsw->askw', coefficient, entry_values, preferred_element_...  3.39 us
  transfers between devices with their start and end apart: 4, of which 2 were waited for; matrix products, arithmetic and copies ran while one was open for 14% of the time, Pallas kernels for 0%

profile of v1, /device:TPU:0, one launch (start us, length us, event | category | flops | bytes accessed | tf_op | source)
XLA Modules:
  0.0 161.0 jit_solution(1739651910366405445)
XLA Ops:
  6.5 4.5 %collective-permute-start = (bf16[1,32,8,2,128]{4,3,2,1,0:T(2,128)(2,1)}, bf16[1,32,8,2,128]{4,3,2,1,0:T(2,128)(2,1)S(1)}, u32[]{:S(2)}, u32[]{:S(2)}) collective-permute-start(bf16[1,32,8,2,128]{4,3,2,1,0:T(2,128)(2,1)} %param.12), channel_id=1, source_target_pairs={{0,28},{4,0},{8,4},{12,8},{16,12},{20,16},{24,20},{28,24},{1,29},{... | collective-permute-start | bytes 393224 | tf_op jit(solution)/shard_map/ppermute | solution.py:12
  12.4 2.0 %fusion.122 = (bf16[1,1,32,2048]{3,2,1,0:T(8,128)(2,1)}, bf16[1,1,32,2048]{3,2,1,0:T(8,128)(2,1)S(1)}, bf16[1,1,32,2048]{3,2,1,0:T(8,128)(2,1)S(1)}, bf16[1,1,32...) fusion(bf16[3,2,32,2048]{3,2,1,0:T(8,128)(2,1)} %bitcast.280), kind=kLoop, calls=%fused_computation.185 | loop fusion | bytes 1572864 | tf_op jit(solution)/shard_map/slice | solution.py:69
  17.0 1.3 convert_bitcast_fusion.1
  20.1 1.2 collective-permute-start.1
  22.0 1.6 %reshape_squeeze.51 = bf16[32,2,1024]{2,1,0:T(2,128)(2,1)} reshape(bf16[1,1,32,2048]{3,2,1,0:T(8,128)(2,1)} %get-tuple-element.22) | data formatting | bytes 262144 | tf_op jit(solution)/shard_map/reshape;squeeze | solution.py:68
  23.6 1.6 %reshape_squeeze.52 = bf16[32,2,1024]{2,1,0:T(2,128)(2,1)} reshape(bf16[1,1,32,2048]{3,2,1,0:T(8,128)(2,1)} %get-tuple-element.17) | data formatting | bytes 262144 | tf_op jit(solution)/shard_map/reshape;squeeze | solution.py:69
  25.2 1.6 %reshape_squeeze.53 = bf16[32,2,1024]{2,1,0:T(2,128)(2,1)} reshape(bf16[1,1,32,2048]{3,2,1,0:T(8,128)(2,1)} %get-tuple-element.16) | data formatting | bytes 262144 | tf_op jit(solution)/shard_map/reshape;squeeze | solution.py:77
  26.9 1.6 %reshape_squeeze.54 = bf16[32,2,1024]{2,1,0:T(2,128)(2,1)} reshape(bf16[1,1,32,2048]{3,2,1,0:T(8,128)(2,1)} %get-tuple-element.11) | data formatting | bytes 262144 | tf_op jit(solution)/shard_map/reshape;squeeze | solution.py:78
  38.4 21.0 %collective-permute-done.2 = bf16[1,32,32,2,128]{4,3,2,1,0:T(2,128)(2,1)S(1)} collective-permute-done((bf16[1,32,32,2,128]{4,3,2,1,0:T(2,128)(2,1)S(1)}, bf16[1,32,32,2,128]{4,3,2,1,0:T(2,128)(2,1)S(1)}, u32[]{:S(2)}, u32[]{:S(2)}) %collective-permute-start.2) | collective-permute-done | bytes 524320 | tf_op jit(solution)/shard_map/ppermute | solution.py:12
  59.3 1.3 constant_dynamic-update-slice_fusion.4
  63.1 1.3 constant_dynamic-update-slice_fusion
  64.3 2.1 %constant_dynamic-slice_fusion.1 = bf16[1,32,64,2,128]{4,3,2,1,0:T(2,128)(2,1)S(1)} fusion(bf16[1,32,128,2,128]{4,3,2,1,0:T(2,128)(2,1)} %constant_dynamic-update-slice_fusion, s32[]{:T(128)S(6)} %select_n.17), kind=kLoop, calls=%fused_computation.178 | loop fusion | bytes 2097156 | tf_op jit(solution)/shard_map/jit(_roll_dynamic)/dynamic_slice | solution.py:16
  71.1 2.0 %fusion.10 = bf16[64,128,16]{1,2,0:T(8,128)(2,1)} fusion(f32[64,128,16]{1,2,0:T(8,128)} %fusion.28, bf16[32,64,2,128]{3,0,1,2:T(8,128)(2,1)S(1)} %bitcast.247, s32[32]{0:T(128)S(1)} %bitcast.299, bf16[32]{0:T(256)(128)(2,1)S(1)} %get-tuple-element.5), kind=kOutput, calls=%fused_computation.22 | convolution fusion | flops 8651776 | bytes 1311744 | tf_op jit(solution)/shard_map/aqk,qsw->askw/dot_general | solution.py:37
  73.0 1.8 %squeeze.88 = bf16[64,2,1024]{2,1,0:T(2,128)(2,1)} reshape(bf16[1,64,16,128]{3,2,1,0:T(8,128)(2,1)} %bitcast.257) | data formatting | bytes 524288 | tf_op jit(solution)/shard_map/squeeze | solution.py:71
  75.8 1.7 %squeeze.94 = bf16[64,4,512]{2,1,0:T(4,128)(2,1)} reshape(bf16[1,64,16,128]{3,2,1,0:T(8,128)(2,1)} %bitcast.259) | data formatting | bytes 524288 | tf_op jit(solution)/shard_map/squeeze | solution.py:71
  77.6 1.8 %squeeze.95 = bf16[64,4,512]{2,1,0:T(4,128)(2,1)} reshape(bf16[1,64,16,128]{3,2,1,0:T(8,128)(2,1)} %bitcast.254) | data formatting | bytes 524288 | tf_op jit(solution)/shard_map/squeeze | solution.py:71
  79.3 1.2 fusion.52
  84.3 1.1 fusion.78
  85.4 1.1 fusion.80
  86.4 1.2 fusion.12
  87.6 1.2 fusion.13
  90.5 1.1 fusion.68
  91.6 1.1 fusion.70
  92.7 1.1 fusion.34
  93.8 1.1 fusion.30
  95.4 8.5 %all_gather.3 = bf16[1,4,64,2,32]{2,4,3,0,1:T(8,128)(2,1)S(1)} all-gather(bf16[1,1,64,2,32]{2,4,3,0,1:T(8,128)(2,1)S(1)} %maximum_bitcast_fusion), channel_id=1, replica_groups=mesh['ang'=8,'row'=4] {'row'}, dimensions={1}, use_global_device_ids=true | all-gather | bytes 40960 | tf_op jit(solution)/shard_map/all_gather | solution.py:129
  106.8 1.2 fusion.19
  111.6 1.5 fusion.2
  117.9 1.6 %subtract_bitcast_fusion = (f32[64,1,2048]{2,0,1:T(8,128)S(1)}, f32[64,1,2048]{2,0,1:T(8,128)S(1)}) fusion(f32[64,2048]{1,0:T(8,128)S(1)} %fusion, f32[]{:T(128)} %bitcast.62, f32[]{:T(128)} %bitcast, f32[64,2048]{1,0:T(8,128)S(1)} %fusion.64, bf16[64,32]{0,1:T(8,128)(2,1)S(1)} %fusion.23, bf16[1,2,32,2048]{3,2,1,0:T(8,128)(2,1)S(1)} %copy-done.4, ...), kind=kOutput, calls=%fused_computation.58 | convolution fusion | flops 9830400 | bytes 4333576 | tf_op jit(solution)/shard_map/rm,sr->sm/dot_general | solution.py:22
  119.6 1.1 pad_maximum_fusion
  120.7 31.9 %reduce-scatter.2.cloned.1.call-done = f32[8,2,2048]{2,0,1:T(8,128)} async-done(((f32[64,2,2048]{2,0,1:T(8,128)}), f32[8,2,2048]{2,0,1:T(8,128)}) %reduce-scatter.2.cloned.1.call-update) | async-done | bytes 131088 | tf_op jit(solution)/shard_map/reduce_scatter | solution.py:159
  152.5 1.7 %copy.140 = f32[8,2,2048]{2,1,0:T(2,128)} copy(f32[8,2,2048]{2,0,1:T(8,128)} %reduce-scatter.2.cloned.1.call-done) | data formatting | bytes 262144 | tf_op jit(solution)/shard_map/reduce_scatter | solution.py:159
  (166 shorter events, 40.4 us)
Async XLA Ops:
  6.5 4.5 %copy-start = (f32[8,2]{0,1:T(2,128)S(1)}, f32[8,2]{0,1:T(2,128)}, u32[]{:S(2)}) copy-start(f32[8,2]{0,1:T(2,128)} %param.15) | copy-start | bytes 196
  6.5 7.8 %copy-start.17 = (bf16[1,3,2,32,2048]{4,3,2,1,0:T(8,128)(2,1)S(1)}, bf16[1,3,2,32,2048]{4,3,2,1,0:T(8,128)(2,1)}, u32[]{:S(2)}) copy-start(bf16[1,3,2,32,2048]{4,3,2,1,0:T(8,128)(2,1)} %param.17) | copy-start | bytes 2359300
  6.5 146.0 %reduce-scatter.2.cloned.1.call-start = ((), (), s32[]{:S(2)}) async-start(), calls=%async_computation.1 | async-start | bytes 1179648 | tf_op jit(solution)/shard_map/reduce_scatter | solution.py:159
  6.5 12.5 %collective-permute-start = (bf16[1,32,8,2,128]{4,3,2,1,0:T(2,128)(2,1)}, bf16[1,32,8,2,128]{4,3,2,1,0:T(2,128)(2,1)S(1)}, u32[]{:S(2)}, u32[]{:S(2)}) collective-permute-start(bf16[1,32,8,2,128]{4,3,2,1,0:T(2,128)(2,1)} %param.12), channel_id=1, source_target_pairs={{0,28},{4,0},{8,4},{12,8},{16,12},{20,16},{24,20},{28,24},{1,29},{... | collective-permute-start | bytes 393224 | tf_op jit(solution)/shard_map/ppermute | solution.py:12
  11.0 4.1 %copy-start.6 = (bf16[1,2,2048,256]{3,2,1,0:T(8,128)(2,1)S(1)}, bf16[1,2,2048,256]{3,2,1,0:T(8,128)(2,1)}, u32[]{:S(2)}) copy-start(bf16[1,2,2048,256]{3,2,1,0:T(8,128)(2,1)} %param.16) | copy-start | bytes 6291460
  15.1 3.2 %copy-start.9 = (bf16[1,32,8,2,128]{4,3,2,1,0:T(2,128)(2,1)S(1)}, bf16[1,32,8,2,128]{4,3,2,1,0:T(2,128)(2,1)}, u32[]{:S(2)}) copy-start(bf16[1,32,8,2,128]{4,3,2,1,0:T(2,128)(2,1)} %param.12) | copy-start | bytes 393220
  15.1 6.3 %copy-start.40 = (f32[1,2]{1,0:T(1,128)S(1)}, f32[1,2]{1,0:T(1,128)}, u32[]{:S(2)}) copy-start(f32[1,2]{1,0:T(1,128)} %param.23) | copy-start | bytes 28
  20.1 15.0 %collective-permute-start.1 = (bf16[1,32,16,2,128]{4,3,2,1,0:T(2,128)(2,1)}, bf16[1,32,16,2,128]{4,3,2,1,0:T(2,128)(2,1)S(1)}, u32[]{:S(2)}, u32[]{:S(2)}) collective-permute-start(bf16[1,32,16,2,128]{4,3,2,1,0:T(2,128)(2,1)} %pad_maximum_fusion.2), channel_id=1, source_target_pairs={{0,24},{4,28},{8,0},{12,4},{16,8},{20,12},{24,16},{28,20},{1,25},{... | collective-permute-start | bytes 786440 | tf_op jit(solution)/shard_map/ppermute | solution.py:12
  35.9 23.4 %collective-permute-start.2 = (bf16[1,32,32,2,128]{4,3,2,1,0:T(2,128)(2,1)S(1)}, bf16[1,32,32,2,128]{4,3,2,1,0:T(2,128)(2,1)S(1)}, u32[]{:S(2)}, u32[]{:S(2)}) collective-permute-start(bf16[1,32,32,2,128]{4,3,2,1,0:T(2,128)(2,1)S(1)} %pad_maximum_fusion.1), channel_id=1, source_target_pairs={{0,16},{4,20},{8,24},{12,28},{16,0},{20,4},{24,8},{28,12},{1,17},{... | collective-permute-start | bytes 1572872 | tf_op jit(solution)/shard_map/ppermute | solution.py:12
  64.3 2.8 %copy-start.39 = (s32[1,32]{1,0:T(1,128)S(1)}, s32[1,32]{1,0:T(1,128)}, u32[]{:S(2)}) copy-start(s32[1,32]{1,0:T(1,128)} %param.13) | copy-start | bytes 388
  73.0 7.5 %copy-start.36 = (bf16[4,8,8,256]{3,2,1,0:T(8,128)(2,1)S(1)}, bf16[4,8,8,256]{3,2,1,0:T(8,128)(2,1)}, u32[]{:S(2)}) copy-start(bf16[4,8,8,256]{3,2,1,0:T(8,128)(2,1)} %copy.151) | copy-start | bytes 393220
  79.3 3.4 %copy-start.26 = (bf16[64,4,512]{2,1,0:T(4,128)(2,1)S(1)}, bf16[64,4,512]{2,1,0:T(4,128)(2,1)}, u32[]{:S(2)}) copy-start(bf16[64,4,512]{2,1,0:T(4,128)(2,1)} %squeeze.94) | copy-start | bytes 786436
  79.3 3.4 %copy-start.35 = (bf16[32,4,512]{2,1,0:T(4,128)(2,1)S(1)}, bf16[32,4,512]{2,1,0:T(4,128)(2,1)}, u32[]{:S(2)}) copy-start(bf16[32,4,512]{2,1,0:T(4,128)(2,1)} %reshape_squeeze.55) | copy-start | bytes 393220
  80.6 2.4 %copy-start.27 = (bf16[64,4,512]{2,1,0:T(4,128)(2,1)S(1)}, bf16[64,4,512]{2,1,0:T(4,128)(2,1)}, u32[]{:S(2)}) copy-start(bf16[64,4,512]{2,1,0:T(4,128)(2,1)} %squeeze.95) | copy-start | bytes 786436
  80.6 2.6 %copy-start.34 = (bf16[32,4,512]{2,1,0:T(4,128)(2,1)S(1)}, bf16[32,4,512]{2,1,0:T(4,128)(2,1)}, u32[]{:S(2)}) copy-start(bf16[32,4,512]{2,1,0:T(4,128)(2,1)} %reshape_squeeze.56) | copy-start | bytes 393220
  82.3 2.0 %copy-start.14 = (bf16[32,4,512]{2,1,0:T(4,128)(2,1)S(1)}, bf16[32,4,512]{2,1,0:T(4,128)(2,1)}, u32[]{:S(2)}) copy-start(bf16[32,4,512]{2,1,0:T(4,128)(2,1)} %reshape_squeeze.57) | copy-start | bytes 393220
  83.4 7.1 %copy-start.13 = (bf16[4,8,8,256]{3,2,1,0:T(8,128)(2,1)S(1)}, bf16[4,8,8,256]{3,2,1,0:T(8,128)(2,1)}, u32[]{:S(2)}) copy-start(bf16[4,8,8,256]{3,2,1,0:T(8,128)(2,1)} %copy.153) | copy-start | bytes 393220
  84.3 8.4 %copy-start.3 = (bf16[64,128,16]{1,2,0:T(8,128)(2,1)S(1)}, bf16[64,128,16]{1,2,0:T(8,128)(2,1)}, u32[]{:S(2)}) copy-start(bf16[64,128,16]{1,2,0:T(8,128)(2,1)} %fusion.10) | copy-start | bytes 786436
  85.4 8.4 %copy-start.2 = (bf16[64,128,16]{1,2,0:T(8,128)(2,1)S(1)}, bf16[64,128,16]{1,2,0:T(8,128)(2,1)}, u32[]{:S(2)}) copy-start(bf16[64,128,16]{1,2,0:T(8,128)(2,1)} %copy-done.1) | copy-start | bytes 786436
  90.4 2.3 %copy-start.15 = (bf16[64,2,4,2,32]{0,4,3,2,1:T(8,128)(2,1)}, bf16[64,2,4,2,32]{0,4,3,2,1:T(8,128)(2,1)S(1)}, u32[]{:S(2)}) copy-start(bf16[64,2,4,2,32]{0,4,3,2,1:T(8,128)(2,1)S(1)} %rev.8) | copy-start | bytes 196612
  90.4 4.5 %copy-start.30 = (bf16[1,2,32,2048]{3,2,1,0:T(8,128)(2,1)S(1)}, bf16[1,2,32,2048]{3,2,1,0:T(8,128)(2,1)}, u32[]{:S(2)}) copy-start(bf16[1,2,32,2048]{3,2,1,0:T(8,128)(2,1)} %get-tuple-element.30) | copy-start | bytes 786436
  90.4 13.5 %copy-start.22 = (bf16[1,1,32,4,32]{4,3,2,1,0:T(4,128)(2,1)S(1)}, bf16[1,1,32,4,32]{4,3,2,1,0:T(4,128)(2,1)}, u32[]{:S(2)}) copy-start(bf16[1,1,32,4,32]{4,3,2,1,0:T(4,128)(2,1)} %get-tuple-element.24) | copy-start | bytes 24580
  90.4 15.1 %copy-start.24 = (bf16[64,2,1024]{2,1,0:T(2,128)(2,1)S(1)}, bf16[64,2,1024]{2,1,0:T(2,128)(2,1)}, u32[]{:S(2)}) copy-start(bf16[64,2,1024]{2,1,0:T(2,128)(2,1)} %squeeze.90) | copy-start | bytes 786436
  90.4 15.1 %copy-start.33 = (bf16[32,2,1024]{2,1,0:T(2,128)(2,1)S(1)}, bf16[32,2,1024]{2,1,0:T(2,128)(2,1)}, u32[]{:S(2)}) copy-start(bf16[32,2,1024]{2,1,0:T(2,128)(2,1)} %reshape_squeeze.51) | copy-start | bytes 393220
  90.4 15.3 %copy-start.25 = (bf16[64,2,1024]{2,1,0:T(2,128)(2,1)S(1)}, bf16[64,2,1024]{2,1,0:T(2,128)(2,1)}, u32[]{:S(2)}) copy-start(bf16[64,2,1024]{2,1,0:T(2,128)(2,1)} %squeeze.88) | copy-start | bytes 786436
  91.6 14.4 %copy-start.32 = (bf16[32,2,1024]{2,1,0:T(2,128)(2,1)S(1)}, bf16[32,2,1024]{2,1,0:T(2,128)(2,1)}, u32[]{:S(2)}) copy-start(bf16[32,2,1024]{2,1,0:T(2,128)(2,1)} %reshape_squeeze.52) | copy-start | bytes 393220
  93.8 14.8 %copy-start.12 = (bf16[32,2,1024]{2,1,0:T(2,128)(2,1)S(1)}, bf16[32,2,1024]{2,1,0:T(2,128)(2,1)}, u32[]{:S(2)}) copy-start(bf16[32,2,1024]{2,1,0:T(2,128)(2,1)} %reshape_squeeze.53) | copy-start | bytes 393220
  95.1 15.4 %copy-start.10 = (bf16[32,2,1024]{2,1,0:T(2,128)(2,1)S(1)}, bf16[32,2,1024]{2,1,0:T(2,128)(2,1)}, u32[]{:S(2)}) copy-start(bf16[32,2,1024]{2,1,0:T(2,128)(2,1)} %reshape_squeeze.54) | copy-start | bytes 393220
  103.9 4.0 %copy-start.18 = (bf16[1,4,64,2,32]{2,4,1,3,0:T(8,128)(2,1)}, bf16[1,4,64,2,32]{2,4,1,3,0:T(8,128)(2,1)S(1)}, u32[]{:S(2)}) copy-start(bf16[1,4,64,2,32]{2,4,1,3,0:T(8,128)(2,1)S(1)} %copy_multiply_fusion) | copy-start | bytes 98308
  111.5 1.7 %copy-start.5 = (f32[4,64,512]{2,1,0:T(8,128)S(1)}, f32[4,64,512]{2,1,0:T(8,128)}, u32[]{:S(2)}) copy-start(f32[4,64,512]{2,1,0:T(8,128)} %fusion.78) | copy-start | bytes 1572868
  111.6 1.7 %copy-start.21 = (bf16[64,2,2,2,32]{0,4,3,2,1:T(8,128)(2,1)S(1)}, bf16[64,2,2,2,32]{0,4,3,2,1:T(8,128)(2,1)}, u32[]{:S(2)}) copy-start(bf16[64,2,2,2,32]{0,4,3,2,1:T(8,128)(2,1)} %copy-done.20) | copy-start | bytes 98308
  115.4 1.7 %copy-start.4 = (bf16[1,2,32,2048]{3,2,1,0:T(8,128)(2,1)S(1)}, bf16[1,2,32,2048]{3,2,1,0:T(8,128)(2,1)}, u32[]{:S(2)}) copy-start(bf16[1,2,32,2048]{3,2,1,0:T(8,128)(2,1)} %get-tuple-element.29) | copy-start | bytes 786436
  (13 other events, 14.3 us)
Sparse Core Ops, SparseCore 0:
  120.8 31.7 reduce-scatter.1
